TPU v7x, 512 devices: a whole 4x8x8 slice. The times are simulated.
512 devices in a mesh: ctx: 128 (over x, z, y_lo, core), head: 4 (over y_hi).
Axes of the slice: x: 4, y: 8 (y_hi: 4, y_lo: 2; y = y_hi * 2 + y_lo), z: 8, core: 2. Of those that a mesh axis runs over, the one named last changes fastest.
Arguments:
- queries: bfloat16 [32768, 2048], P('ctx', 'head'), may hold values from -8 to 8
- keys: bfloat16 [32768, 2048], P('ctx', 'head'), may hold values from -8 to 8
- values: bfloat16 [32768, 2048], P('ctx', 'head'), may hold values from -6 to 6
- out_grad: bfloat16 [32768, 2048], P('ctx', 'head'), may hold values from -6 to 6
Outputs:
- attended: bfloat16 [32768, 2048], P('ctx', 'head')
- query_grad: bfloat16 [32768, 2048], P('ctx', 'head')
- key_grad: bfloat16 [32768, 2048], P('ctx', 'head')
- value_grad: bfloat16 [32768, 2048], P('ctx', 'head')
All inputs are finite; a program needn't handle non-finite values.
Results may differ from a plain program's by a relative error of at most 0.017.
Values may be sent and summed in bfloat16 or wider, within the bound.
No kernel may reach another device: no remote copies, remote signals or barrier semaphores. Data moves between devices by JAX's collectives and lax.ppermute only.
A program may use at most 64 MiB of HBM per device.

v0:
```python
import math
import jax
import jax.numpy as jnp
from jax import lax
from jax.sharding import PartitionSpec as P

HD = 128
STRIDE = 128
SUMMARY = 4


def split_heads(matrix):
    blocks = matrix.shape[0] // STRIDE
    half_heads = matrix.shape[1] // (2 * HD)
    shaped = matrix.reshape(blocks, STRIDE, matrix.shape[1] // (4 * HD), 4, HD)
    fixed = shaped[:, :, :, :2].reshape(blocks, STRIDE, half_heads, HD)
    strided = shaped[:, :, :, 2:].reshape(blocks, STRIDE, half_heads, HD)
    return (fixed, strided)


def join_heads(fixed, strided):
    blocks, positions, half_heads, head_dim = fixed.shape
    paired = jnp.concatenate(
        [
            fixed.reshape(blocks, positions, half_heads // 2, 2, head_dim),
            strided.reshape(blocks, positions, half_heads // 2, 2, head_dim),
        ],
        axis=3,
    )
    return paired.reshape(blocks * positions, 2 * half_heads * head_dim)


def fixed_heads(query, key_rows, value_rows, grad_rows, scaling):
    blocks_here, positions, half_heads, head_dim = query.shape
    summary_keys = key_rows[:, positions - SUMMARY :]
    summary_values = value_rows[:, positions - SUMMARY :]
    every_key, every_value = (
        lax.all_gather(summary_keys, "ctx", axis=0, tiled=True),
        lax.all_gather(summary_values, "ctx", axis=0, tiled=True),
    )
    summary_count = every_key.shape[0] * SUMMARY
    flat_keys = every_key.reshape(summary_count, half_heads, head_dim)
    flat_values = every_value.reshape(summary_count, half_heads, head_dim)
    block_ids = lax.axis_index("ctx") * blocks_here + jnp.arange(blocks_here, dtype=jnp.int32)
    summary_block = jnp.arange(summary_count, dtype=jnp.int32) // SUMMARY
    earlier = (summary_block[None, :] < block_ids[:, None])[:, None, None, :]
    causal = (jnp.arange(positions)[:, None] >= jnp.arange(positions)[None, :])[None, None]
    local_scores = (
        jnp.einsum("bqgd,bkgd->bgqk", query, key_rows, preferred_element_type=jnp.float32) * scaling
    )
    summary_scores = (
        jnp.einsum("bqgd,mgd->bgqm", query, flat_keys, preferred_element_type=jnp.float32) * scaling
    )
    local_scores = jnp.where(causal, local_scores, -jnp.inf)
    summary_scores = jnp.where(earlier, summary_scores, -jnp.inf)
    row_max = jnp.maximum(jnp.max(local_scores, axis=-1), jnp.max(summary_scores, axis=-1))[
        ..., None
    ]
    local_raised = jnp.exp(local_scores - row_max)
    summary_raised = jnp.exp(summary_scores - row_max)
    totals = jnp.sum(local_raised, axis=-1, keepdims=True) + jnp.sum(
        summary_raised, axis=-1, keepdims=True
    )
    local_weights = local_raised / totals
    summary_weights = summary_raised / totals
    local_low = local_weights.astype(jnp.bfloat16)
    summary_low = summary_weights.astype(jnp.bfloat16)
    attended = (
        jnp.einsum("bgqk,bkgd->bqgd", local_low, value_rows, preferred_element_type=jnp.float32)
        + jnp.einsum("bgqm,mgd->bqgd", summary_low, flat_values, preferred_element_type=jnp.float32)
    ).astype(jnp.bfloat16)
    local_dweights = jnp.einsum(
        "bqgd,bkgd->bgqk", grad_rows, value_rows, preferred_element_type=jnp.float32
    )
    summary_dweights = jnp.einsum(
        "bqgd,mgd->bgqm", grad_rows, flat_values, preferred_element_type=jnp.float32
    )
    row_delta = jnp.sum(grad_rows.astype(jnp.float32) * attended.astype(jnp.float32), axis=-1)
    row_delta = jnp.transpose(row_delta, (0, 2, 1))[..., None]
    local_dscores = (local_weights * (local_dweights - row_delta)).astype(jnp.bfloat16)
    summary_dscores = (summary_weights * (summary_dweights - row_delta)).astype(jnp.bfloat16)
    query_grad = (
        jnp.einsum("bgqk,bkgd->bqgd", local_dscores, key_rows, preferred_element_type=jnp.float32)
        + jnp.einsum(
            "bgqm,mgd->bqgd", summary_dscores, flat_keys, preferred_element_type=jnp.float32
        )
    ) * scaling
    key_grad = (
        jnp.einsum("bgqk,bqgd->bkgd", local_dscores, query, preferred_element_type=jnp.float32)
        * scaling
    )
    value_grad = jnp.einsum(
        "bgqk,bqgd->bkgd", local_low, grad_rows, preferred_element_type=jnp.float32
    )
    key_terms = (
        jnp.einsum("bgqm,bqgd->mgd", summary_dscores, query, preferred_element_type=jnp.float32)
        * scaling
    )
    value_terms = jnp.einsum(
        "bgqm,bqgd->mgd", summary_low, grad_rows, preferred_element_type=jnp.float32
    )
    shares = lax.psum_scatter(
        jnp.stack([key_terms, value_terms], axis=1), "ctx", scatter_dimension=0, tiled=True
    )
    shares = shares.reshape(blocks_here, SUMMARY, 2, half_heads, head_dim)
    key_grad = key_grad.at[:, positions - SUMMARY :].add(shares[:, :, 0])
    value_grad = value_grad.at[:, positions - SUMMARY :].add(shares[:, :, 1])
    return (
        attended,
        query_grad.astype(jnp.bfloat16),
        key_grad.astype(jnp.bfloat16),
        value_grad.astype(jnp.bfloat16),
    )


def strided_heads(query, key_rows, value_rows, grad_rows, scaling):
    query_all = lax.all_to_all(query, "ctx", split_axis=1, concat_axis=0, tiled=True)
    keys_all = lax.all_to_all(key_rows, "ctx", split_axis=1, concat_axis=0, tiled=True)
    values_all = lax.all_to_all(value_rows, "ctx", split_axis=1, concat_axis=0, tiled=True)
    grads_all = lax.all_to_all(grad_rows, "ctx", split_axis=1, concat_axis=0, tiled=True)
    blocks = query_all.shape[0]
    causal = (jnp.arange(blocks)[:, None] >= jnp.arange(blocks)[None, :])[None, None]
    scores = (
        jnp.einsum("brgd,crgd->rgbc", query_all, keys_all, preferred_element_type=jnp.float32)
        * scaling
    )
    scores = jnp.where(causal, scores, -jnp.inf)
    row_max = jnp.max(scores, axis=-1, keepdims=True)
    raised = jnp.exp(scores - row_max)
    weights = raised / jnp.sum(raised, axis=-1, keepdims=True)
    weights_low = weights.astype(jnp.bfloat16)
    attended = jnp.einsum(
        "rgbc,crgd->brgd", weights_low, values_all, preferred_element_type=jnp.float32
    ).astype(jnp.bfloat16)
    dweights = jnp.einsum(
        "brgd,crgd->rgbc", grads_all, values_all, preferred_element_type=jnp.float32
    )
    row_delta = jnp.sum(grads_all.astype(jnp.float32) * attended.astype(jnp.float32), axis=-1)
    row_delta = jnp.transpose(row_delta, (1, 2, 0))[..., None]
    dscores = (weights * (dweights - row_delta)).astype(jnp.bfloat16)
    query_grad = (
        jnp.einsum("rgbc,crgd->brgd", dscores, keys_all, preferred_element_type=jnp.float32)
        * scaling
    ).astype(jnp.bfloat16)
    key_grad = (
        jnp.einsum("rgbc,brgd->crgd", dscores, query_all, preferred_element_type=jnp.float32)
        * scaling
    ).astype(jnp.bfloat16)
    value_grad = jnp.einsum(
        "rgbc,brgd->crgd", weights_low, grads_all, preferred_element_type=jnp.float32
    ).astype(jnp.bfloat16)
    return (
        lax.all_to_all(attended, "ctx", split_axis=0, concat_axis=1, tiled=True),
        lax.all_to_all(query_grad, "ctx", split_axis=0, concat_axis=1, tiled=True),
        lax.all_to_all(key_grad, "ctx", split_axis=0, concat_axis=1, tiled=True),
        lax.all_to_all(value_grad, "ctx", split_axis=0, concat_axis=1, tiled=True),
    )


def shards(queries, keys, values, out_grad):
    scaling = 1.0 / math.sqrt(HD)
    query_fixed, query_strided = split_heads(queries)
    key_fixed, key_strided = split_heads(keys)
    value_fixed, value_strided = split_heads(values)
    grad_fixed, grad_strided = split_heads(out_grad)
    fixed_out = fixed_heads(query_fixed, key_fixed, value_fixed, grad_fixed, scaling)
    strided_out = strided_heads(query_strided, key_strided, value_strided, grad_strided, scaling)
    return (
        join_heads(fixed_out[0], strided_out[0]),
        join_heads(fixed_out[1], strided_out[1]),
        join_heads(fixed_out[2], strided_out[2]),
        join_heads(fixed_out[3], strided_out[3]),
    )


def solution(mesh):
    return jax.shard_map(
        shards,
        mesh=mesh,
        in_specs=(P("ctx", "head"), P("ctx", "head"), P("ctx", "head"), P("ctx", "head")),
        out_specs=(P("ctx", "head"), P("ctx", "head"), P("ctx", "head"), P("ctx", "head")),
        check_vma=False,
    )
```

profile of v0, /device:TPU:16, one launch (start us, length us, event | category | flops | bytes accessed | tf_op | source)
XLA Modules:
  0.0 909.7 jit_solution(8492532768877551417)
XLA Ops:
  11.0 165.1 %all_gather.7 = bf16[256,4,2,128]{3,1,2,0:T(4,128)(2,1)S(1)} all-gather(bf16[2,4,2,128]{3,1,2,0:T(4,128)(2,1)S(1)} %copy.203), channel_id=1, replica_groups=mesh['ctx'=128,'head'=4] {'ctx'}, dimensions={0}, use_global_device_ids=true | all-gather | bytes 528384 | tf_op jit(solution)/shard_map/all_gather | solution.py:39
  176.2 153.2 %all_gather.6 = bf16[256,4,2,128]{3,1,2,0:T(4,128)(2,1)S(1)} all-gather(bf16[2,4,2,128]{3,1,2,0:T(4,128)(2,1)S(1)} %slice.111), channel_id=1, replica_groups=mesh['ctx'=128,'head'=4] {'ctx'}, dimensions={0}, use_global_device_ids=true | all-gather | bytes 528384 | tf_op jit(solution)/shard_map/all_gather | solution.py:38
  333.8 1.5 pad_maximum_fusion
  336.1 6.2 all-to-all-start
  343.0 10.3 %all-to-all-done = bf16[2,128,2,128]{3,2,0,1:T(2,128)(2,1)S(1)} async-done(((bf16[2,128,2,128]{3,2,0,1:T(2,128)(2,1)}), bf16[2,128,2,128]{3,2,0,1:T(2,128)(2,1)S(1)}, u32[]{:S(2)}, u32[]{:S(2)}) %all-to-all-start) | async-done | bytes 131104 | tf_op jit(solution)/shard_map/all_to_all | solution.py:117
  353.3 6.2 all-to-all-start.1
  360.2 10.3 %all-to-all-done.1 = bf16[2,128,2,128]{3,2,0,1:T(2,128)(2,1)S(1)} async-done(((bf16[2,128,2,128]{3,2,0,1:T(2,128)(2,1)}), bf16[2,128,2,128]{3,2,0,1:T(2,128)(2,1)S(1)}, u32[]{:S(2)}, u32[]{:S(2)}) %all-to-all-start.1) | async-done | bytes 131104 | tf_op jit(solution)/shard_map/all_to_all | solution.py:118
  370.6 6.4 all-to-all-start.2
  377.7 10.2 %all-to-all-done.2 = bf16[2,128,2,128]{3,2,0,1:T(2,128)(2,1)S(1)} async-done(((bf16[2,128,2,128]{3,2,0,1:T(2,128)(2,1)}), bf16[2,128,2,128]{3,2,0,1:T(2,128)(2,1)S(1)}, u32[]{:S(2)}, u32[]{:S(2)}) %all-to-all-start.2) | async-done | bytes 131104 | tf_op jit(solution)/shard_map/all_to_all | solution.py:119
  387.9 6.2 all-to-all-start.4
  394.9 10.2 %all-to-all-done.4 = bf16[2,128,2,128]{3,2,0,1:T(2,128)(2,1)S(1)} async-done(((bf16[2,128,2,128]{3,2,0,1:T(2,128)(2,1)}), bf16[2,128,2,128]{3,2,0,1:T(2,128)(2,1)S(1)}, u32[]{:S(2)}, u32[]{:S(2)}) %all-to-all-start.4) | async-done | bytes 131104 | tf_op jit(solution)/shard_map/all_to_all | solution.py:120
  405.7 2.0 fusion.64
  407.7 1.3 multiply_reduce_fusion
  409.0 1.3 fusion.11
  411.3 6.2 all-to-all-start.6
  418.8 9.7 %all-to-all-done.6 = bf16[256,1,2,128]{3,2,1,0:T(2,128)(2,1)S(1)} async-done(((bf16[256,1,2,128]{3,2,1,0:T(2,128)(2,1)}), bf16[256,1,2,128]{3,2,1,0:T(2,128)(2,1)S(1)}, u32[]{:S(2)}, u32[]{:S(2)}) %all-to-all-start.6) | async-done | bytes 131104 | tf_op jit(solution)/shard_map/all_to_all | solution.py:155
  428.5 6.2 all-to-all-start.5
  434.9 1.3 fusion.24
  436.9 8.8 all-to-all-done.5
  445.7 6.4 all-to-all-start.7
  453.4 9.7 %all-to-all-done.7 = bf16[256,1,2,128]{3,2,1,0:T(2,128)(2,1)S(1)} async-done(((bf16[256,1,2,128]{3,2,1,0:T(2,128)(2,1)}), bf16[256,1,2,128]{3,2,1,0:T(2,128)(2,1)S(1)}, u32[]{:S(2)}, u32[]{:S(2)}) %all-to-all-start.7) | async-done | bytes 131104 | tf_op jit(solution)/shard_map/all_to_all | solution.py:156
  463.2 6.2 all-to-all-start.3
  470.0 10.4 %all-to-all-done.3 = bf16[256,1,2,128]{3,2,1,0:T(2,128)(2,1)S(1)} async-done(((bf16[256,1,2,128]{3,2,1,0:T(2,128)(2,1)}), bf16[256,1,2,128]{3,2,1,0:T(2,128)(2,1)S(1)}, u32[]{:S(2)}, u32[]{:S(2)}) %all-to-all-start.3) | async-done | bytes 131104 | tf_op jit(solution)/shard_map/all_to_all | solution.py:153
  481.9 417.3 %reduce-scatter.2.cloned.1.call-done = f32[8,2,2,128]{3,0,2,1:T(8,128)} async-done(((f32[1024,2,2,128]{3,0,2,1:T(8,128)}), f32[8,2,2,128]{3,0,2,1:T(8,128)}) %reduce-scatter.2.cloned.1.call-update) | async-done | bytes 16400 | tf_op jit(solution)/shard_map/reduce_scatter | solution.py:102
  (93 shorter events, 22.9 us)
Async XLA Ops:
  7.2 2.9 copy-start
  7.2 3.2 copy-start.1
  7.2 892.0 %reduce-scatter.2.cloned.1.call-start = ((), (), s32[]{:S(2)}) async-start(), calls=%async_computation.9 | async-start | bytes 2113536 | tf_op jit(solution)/shard_map/reduce_scatter | solution.py:102
  336.1 17.2 %all-to-all-start = ((bf16[2,128,2,128]{3,2,0,1:T(2,128)(2,1)}), bf16[2,128,2,128]{3,2,0,1:T(2,128)(2,1)S(1)}, u32[]{:S(2)}, u32[]{:S(2)}) async-start(bf16[2,128,2,128]{3,2,0,1:T(2,128)(2,1)} %copy.207), calls=%async_computation | async-start | bytes 262144 | tf_op jit(solution)/shard_map/all_to_all | solution.py:117
  353.3 17.3 %all-to-all-start.1 = ((bf16[2,128,2,128]{3,2,0,1:T(2,128)(2,1)}), bf16[2,128,2,128]{3,2,0,1:T(2,128)(2,1)S(1)}, u32[]{:S(2)}, u32[]{:S(2)}) async-start(bf16[2,128,2,128]{3,2,0,1:T(2,128)(2,1)} %copy.209), calls=%async_computation.1 | async-start | bytes 262144 | tf_op jit(solution)/shard_map/all_to_all | solution.py:118
  370.6 17.3 %all-to-all-start.2 = ((bf16[2,128,2,128]{3,2,0,1:T(2,128)(2,1)}), bf16[2,128,2,128]{3,2,0,1:T(2,128)(2,1)S(1)}, u32[]{:S(2)}, u32[]{:S(2)}) async-start(bf16[2,128,2,128]{3,2,0,1:T(2,128)(2,1)} %copy.211), calls=%async_computation.2 | async-start | bytes 262144 | tf_op jit(solution)/shard_map/all_to_all | solution.py:119
  387.9 17.3 %all-to-all-start.4 = ((bf16[2,128,2,128]{3,2,0,1:T(2,128)(2,1)}), bf16[2,128,2,128]{3,2,0,1:T(2,128)(2,1)S(1)}, u32[]{:S(2)}, u32[]{:S(2)}) async-start(bf16[2,128,2,128]{3,2,0,1:T(2,128)(2,1)} %copy.227), calls=%async_computation.4 | async-start | bytes 262144 | tf_op jit(solution)/shard_map/all_to_all | solution.py:120
  405.7 4.6 copy-start.2
  410.5 24.4 %copy-start.3 = (bf16[128,2,1,2,128]{4,1,0,3,2:T(2,128)(2,1)S(1)}, bf16[128,2,1,2,128]{4,1,0,3,2:T(2,128)(2,1)}, u32[]{:S(2)}) copy-start(bf16[128,2,1,2,128]{4,1,0,3,2:T(2,128)(2,1)} %copy-done.2) | copy-start | bytes 393220
  411.3 17.2 %all-to-all-start.6 = ((bf16[256,1,2,128]{3,2,1,0:T(2,128)(2,1)}), bf16[256,1,2,128]{3,2,1,0:T(2,128)(2,1)S(1)}, u32[]{:S(2)}, u32[]{:S(2)}) async-start(bf16[256,1,2,128]{3,2,1,0:T(2,128)(2,1)} %copy.242), calls=%async_computation.7 | async-start | bytes 262144 | tf_op jit(solution)/shard_map/all_to_all | solution.py:155
  428.5 17.3 %all-to-all-start.5 = ((bf16[256,1,2,128]{3,2,1,0:T(2,128)(2,1)}), bf16[256,1,2,128]{3,2,1,0:T(2,128)(2,1)S(1)}, u32[]{:S(2)}, u32[]{:S(2)}) async-start(bf16[256,1,2,128]{3,2,1,0:T(2,128)(2,1)} %copy.234), calls=%async_computation.5 | async-start | bytes 262144 | tf_op jit(solution)/shard_map/all_to_all | solution.py:154
  445.7 17.4 %all-to-all-start.7 = ((bf16[256,1,2,128]{3,2,1,0:T(2,128)(2,1)}), bf16[256,1,2,128]{3,2,1,0:T(2,128)(2,1)S(1)}, u32[]{:S(2)}, u32[]{:S(2)}) async-start(bf16[256,1,2,128]{3,2,1,0:T(2,128)(2,1)} %copy.248), calls=%async_computation.8 | async-start | bytes 262144 | tf_op jit(solution)/shard_map/all_to_all | solution.py:156
  453.4 27.4 %copy-start.4 = (bf16[2,128,2,128]{1,3,2,0:T(8,128)(2,1)S(1)}, bf16[2,128,2,128]{1,3,2,0:T(8,128)(2,1)}, u32[]{:S(2)}) copy-start(bf16[2,128,2,128]{1,3,2,0:T(8,128)(2,1)} %get-tuple-element.49) | copy-start | bytes 393220
  463.2 17.3 %all-to-all-start.3 = ((bf16[256,1,2,128]{3,2,1,0:T(2,128)(2,1)}), bf16[256,1,2,128]{3,2,1,0:T(2,128)(2,1)S(1)}, u32[]{:S(2)}, u32[]{:S(2)}) async-start(bf16[256,1,2,128]{3,2,1,0:T(2,128)(2,1)} %copy.215), calls=%async_computation.3 | async-start | bytes 262144 | tf_op jit(solution)/shard_map/all_to_all | solution.py:153
Sparse Core Ops, SparseCore 0:
  335.5 563.6 reduce-scatter.1
where the time goes:
time: 911 us; the launch traced here: 910 us
  waiting for transfers between devices  497 us (55%)
  blocking collectives  318 us (35%)
  starting transfers between devices  49.8 us (5%)
  local copies, waits for them, and re-layouts  15.7 us (2%)
  between operations  14.6 us (2%)
  matrix products  11.1 us (1%)
    reduce_scatter x1, waiting for transfers between devices, fixed_heads(): lax.psum_scatter(jnp.stack([key_terms, value_terms], axis=1), 'ctx', scat...  417 us
    all_gather x1, blocking collectives, fixed_heads(): lax.all_gather(summary_values, 'ctx', axis=0, tiled=True)  165 us
    all_gather x1, blocking collectives, fixed_heads(): lax.all_gather(summary_keys, 'ctx', axis=0, tiled=True)  153 us
  transfers between devices with their start and end apart: 9, of which 9 were waited for; matrix products, arithmetic and copies ran while one was open for 2% of the time, Pallas kernels for 0%

commit v1 on v0

--- a/solution.py
+++ b/solution.py
@@ -7,6 +7,11 @@
 HD = 128
 STRIDE = 128
 SUMMARY = 4
+
+
+def all_by_exchange(x, mesh_axis, dim):
+    outgoing = jnp.stack([x] * lax.axis_size(mesh_axis))
+    return jnp.concatenate(lax.all_to_all(outgoing, mesh_axis, 0, 0), axis=dim)
 
 
 def split_heads(matrix):
@@ -36,7 +41,7 @@
     summary_values = value_rows[:, positions - SUMMARY :]
     every_key, every_value = (
         lax.all_gather(summary_keys, "ctx", axis=0, tiled=True),
-        lax.all_gather(summary_values, "ctx", axis=0, tiled=True),
+        all_by_exchange(summary_values, "ctx", 0),
     )
     summary_count = every_key.shape[0] * SUMMARY
     flat_keys = every_key.reshape(summary_count, half_heads, head_dim)

time: 911 us -> 804 us (0.88)
  blocking collectives: 318 us -> 159 us
  waiting for transfers between devices: 497 us -> 528 us
  starting transfers between devices: 49.8 us -> 67.4 us
    all_gather x1 -> x0, blocking collectives: 165 us -> none  [fixed_heads(): lax.all_gather(summary_values, 'ctx', axis=0, tiled=True)]
    reduce_scatter x1, waiting for transfers between devices: 417 us -> 453 us  [fixed_heads(): lax.psum_scatter(jnp.stack([key_terms, value_terms], axis=1), 'ctx', scat...]
    all_to_all x0 -> x1, starting transfers between devices: none -> 16.6 us  [all_by_exchange(): return jnp.concatenate(lax.all_to_all(outgoing, mesh_axis, 0, 0), axis=dim)]
  transfers between devices with their start and end apart: 9 -> 10, of which waited for: 9 -> 9; matrix products, arithmetic and copies ran while one was open for 2% -> 3% of each run, Pallas kernels for 0% -> 0%
where the time goes in v1:
time: 804 us; the launch traced here: 803 us
  waiting for transfers between devices  528 us (66%)
  blocking collectives  159 us (20%)
  starting transfers between devices  67.4 us (8%)
  local copies, waits for them, and re-layouts  21.2 us (3%)
  between operations  14.8 us (2%)
  matrix products  8.9 us (1%)
    reduce_scatter x1, waiting for transfers between devices, fixed_heads(): lax.psum_scatter(jnp.stack([key_terms, value_terms], axis=1), 'ctx', scat...  453 us
    all_gather x1, blocking collectives, fixed_heads(): lax.all_gather(summary_keys, 'ctx', axis=0, tiled=True)  159 us
    all_to_all x1, starting transfers between devices, all_by_exchange(): return jnp.concatenate(lax.all_to_all(outgoing, mesh_axis, 0, 0), axis=dim)  16.6 us
  transfers between devices with their start and end apart: 10, of which 9 were waited for; matrix products, arithmetic and copies ran while one was open for 3% of the time, Pallas kernels for 0%

profile of v1, /device:TPU:16, one launch (start us, length us, event | category | flops | bytes accessed | tf_op | source)
XLA Modules:
  0.0 803.0 jit_solution(7046625186271416631)
XLA Ops:
  10.4 16.6 %all-to-all-start = ((bf16[128,2,4,2,128]{4,2,1,3,0:T(4,128)(2,1)}), bf16[128,2,4,2,128]{4,2,1,3,0:T(4,128)(2,1)}, u32[]{:S(2)}, u32[]{:S(2)}) async-start(bf16[128,2,4,2,128]{4,2,1,3,0:T(4,128)(2,1)} %stack.8), calls=%async_computation | async-start | bytes 1048576 | tf_op jit(solution)/shard_map/all_to_all | solution.py:14
  28.6 158.9 %all_gather.3 = bf16[256,4,2,128]{3,1,2,0:T(4,128)(2,1)S(1)} all-gather(bf16[2,4,2,128]{3,1,2,0:T(4,128)(2,1)S(1)} %slice.111), channel_id=1, replica_groups=mesh['ctx'=128,'head'=4] {'ctx'}, dimensions={0}, use_global_device_ids=true | all-gather | bytes 528384 | tf_op jit(solution)/shard_map/all_gather | solution.py:43
  193.2 1.4 convolution_bitcast_fusion
  194.6 7.2 all-to-all-start.1
  201.9 1.3 copy.205
  206.0 6.5 all-to-all-done.1
  212.6 6.4 all-to-all-start.2
  219.0 1.5 pad_maximum_fusion
  222.1 7.8 all-to-all-done.2
  229.9 6.2 all-to-all-start.3
  236.8 10.3 %all-to-all-done.3 = bf16[2,128,2,128]{3,2,0,1:T(2,128)(2,1)S(1)} async-done(((bf16[2,128,2,128]{3,2,0,1:T(2,128)(2,1)}), bf16[2,128,2,128]{3,2,0,1:T(2,128)(2,1)S(1)}, u32[]{:S(2)}, u32[]{:S(2)}) %all-to-all-start.3) | async-done | bytes 131104 | tf_op jit(solution)/shard_map/all_to_all | solution.py:124
  247.1 6.2 all-to-all-start.5
  254.4 9.9 %all-to-all-done.5 = bf16[2,128,2,128]{3,2,0,1:T(2,128)(2,1)S(1)} async-done(((bf16[2,128,2,128]{3,2,0,1:T(2,128)(2,1)}), bf16[2,128,2,128]{3,2,0,1:T(2,128)(2,1)S(1)}, u32[]{:S(2)}, u32[]{:S(2)}) %all-to-all-start.5) | async-done | bytes 131104 | tf_op jit(solution)/shard_map/all_to_all | solution.py:125
  266.7 6.2 all-to-all-start.7
  274.0 9.9 %all-to-all-done.7 = bf16[256,1,2,128]{3,2,1,0:T(2,128)(2,1)S(1)} async-done(((bf16[256,1,2,128]{3,2,1,0:T(2,128)(2,1)}), bf16[256,1,2,128]{3,2,1,0:T(2,128)(2,1)S(1)}, u32[]{:S(2)}, u32[]{:S(2)}) %all-to-all-start.7) | async-done | bytes 131104 | tf_op jit(solution)/shard_map/all_to_all | solution.py:160
  283.9 6.2 all-to-all-start.6
  291.1 9.9 %all-to-all-done.6 = bf16[256,1,2,128]{3,2,1,0:T(2,128)(2,1)S(1)} async-done(((bf16[256,1,2,128]{3,2,1,0:T(2,128)(2,1)}), bf16[256,1,2,128]{3,2,1,0:T(2,128)(2,1)S(1)}, u32[]{:S(2)}, u32[]{:S(2)}) %all-to-all-start.6) | async-done | bytes 131104 | tf_op jit(solution)/shard_map/all_to_all | solution.py:159
  301.1 6.4 all-to-all-start.8
  308.3 10.2 %all-to-all-done.8 = bf16[256,1,2,128]{3,2,1,0:T(2,128)(2,1)S(1)} async-done(((bf16[256,1,2,128]{3,2,1,0:T(2,128)(2,1)}), bf16[256,1,2,128]{3,2,1,0:T(2,128)(2,1)S(1)}, u32[]{:S(2)}, u32[]{:S(2)}) %all-to-all-start.8) | async-done | bytes 131104 | tf_op jit(solution)/shard_map/all_to_all | solution.py:161
  318.5 6.2 all-to-all-start.4
  325.1 10.5 %all-to-all-done.4 = bf16[256,1,2,128]{3,2,1,0:T(2,128)(2,1)S(1)} async-done(((bf16[256,1,2,128]{3,2,1,0:T(2,128)(2,1)}), bf16[256,1,2,128]{3,2,1,0:T(2,128)(2,1)S(1)}, u32[]{:S(2)}, u32[]{:S(2)}) %all-to-all-start.4) | async-done | bytes 131104 | tf_op jit(solution)/shard_map/all_to_all | solution.py:158
  335.8 1.1 fusion.20
  339.3 453.1 %reduce-scatter.2.cloned.1.call-done = f32[8,2,2,128]{3,0,2,1:T(8,128)} async-done(((f32[1024,2,2,128]{3,0,2,1:T(8,128)}), f32[8,2,2,128]{3,0,2,1:T(8,128)}) %reduce-scatter.2.cloned.1.call-update) | async-done | bytes 16400 | tf_op jit(solution)/shard_map/reduce_scatter | solution.py:107
  793.7 1.2 scatter-add.6
  (121 shorter events, 27.1 us)
Async XLA Ops:
  7.2 19.9 %copy-start.8 = (bf16[256,512]{1,0:T(8,128)(2,1)S(1)}, bf16[256,512]{1,0:T(8,128)(2,1)}, u32[]{:S(2)}) copy-start(bf16[256,512]{1,0:T(8,128)(2,1)} %param.8) | copy-start | bytes 786436
  7.2 20.1 %copy-start.9 = (bf16[256,512]{1,0:T(8,128)(2,1)S(1)}, bf16[256,512]{1,0:T(8,128)(2,1)}, u32[]{:S(2)}) copy-start(bf16[256,512]{1,0:T(8,128)(2,1)} %param.9) | copy-start | bytes 786436
  9.2 17.8 %copy-start.3 = (bf16[2,128,1,2,128]{1,4,3,0,2:T(8,128)(2,1)}, bf16[2,128,1,2,128]{1,4,3,0,2:T(8,128)(2,1)S(1)}, u32[]{:S(2)}) copy-start(bf16[2,128,1,2,128]{1,4,3,0,2:T(8,128)(2,1)S(1)} %copy.286) | copy-start | bytes 393220
  9.3 18.3 %copy-start.10 = (bf16[256,512]{1,0:T(8,128)(2,1)S(1)}, bf16[256,512]{1,0:T(8,128)(2,1)}, u32[]{:S(2)}) copy-start(bf16[256,512]{1,0:T(8,128)(2,1)} %param.11) | copy-start | bytes 786436
  10.4 184.2 %all-to-all-start = ((bf16[128,2,4,2,128]{4,2,1,3,0:T(4,128)(2,1)}), bf16[128,2,4,2,128]{4,2,1,3,0:T(4,128)(2,1)}, u32[]{:S(2)}, u32[]{:S(2)}) async-start(bf16[128,2,4,2,128]{4,2,1,3,0:T(4,128)(2,1)} %stack.8), calls=%async_computation | async-start | bytes 1048576 | tf_op jit(solution)/shard_map/all_to_all | solution.py:14
  187.6 1.8 copy-start.1
  194.6 17.9 %all-to-all-start.1 = ((bf16[2,128,2,128]{3,2,0,1:T(2,128)(2,1)}), bf16[2,128,2,128]{3,2,0,1:T(2,128)(2,1)}, u32[]{:S(2)}, u32[]{:S(2)}) async-start(bf16[2,128,2,128]{3,2,0,1:T(2,128)(2,1)} %copy.208), calls=%async_computation.1 | async-start | bytes 262144 | tf_op jit(solution)/shard_map/all_to_all | solution.py:122
  201.9 1.7 copy-start.4
  201.9 1.7 copy-start.11
  205.6 13.4 %copy-start = (f32[1024,1,2,128]{3,0,2,1:T(8,128)S(1)}, f32[1024,1,2,128]{3,0,2,1:T(8,128)}, u32[]{:S(2)}) copy-start(f32[1024,1,2,128]{3,0,2,1:T(8,128)} %convolution_bitcast_fusion) | copy-start | bytes 3145732
  212.6 17.3 %all-to-all-start.2 = ((bf16[2,128,2,128]{3,2,0,1:T(2,128)(2,1)}), bf16[2,128,2,128]{3,2,0,1:T(2,128)(2,1)S(1)}, u32[]{:S(2)}, u32[]{:S(2)}) async-start(bf16[2,128,2,128]{3,2,0,1:T(2,128)(2,1)} %copy.210), calls=%async_computation.2 | async-start | bytes 262144 | tf_op jit(solution)/shard_map/all_to_all | solution.py:123
  218.9 573.5 %reduce-scatter.2.cloned.1.call-start = ((), (), s32[]{:S(2)}) async-start(), calls=%async_computation.10 | async-start | bytes 2113536 | tf_op jit(solution)/shard_map/reduce_scatter | solution.py:107
  220.4 15.6 %copy-start.7 = (bf16[2,128,2,128]{3,2,1,0:T(2,128)(2,1)S(1)}, bf16[2,128,2,128]{3,2,1,0:T(2,128)(2,1)}, u32[]{:S(2)}) copy-start(bf16[2,128,2,128]{3,2,1,0:T(2,128)(2,1)} %get-tuple-element.29) | copy-start | bytes 393220
  229.9 17.2 %all-to-all-start.3 = ((bf16[2,128,2,128]{3,2,0,1:T(2,128)(2,1)}), bf16[2,128,2,128]{3,2,0,1:T(2,128)(2,1)S(1)}, u32[]{:S(2)}, u32[]{:S(2)}) async-start(bf16[2,128,2,128]{3,2,0,1:T(2,128)(2,1)} %copy.212), calls=%async_computation.3 | async-start | bytes 262144 | tf_op jit(solution)/shard_map/all_to_all | solution.py:124
  247.1 17.2 %all-to-all-start.5 = ((bf16[2,128,2,128]{3,2,0,1:T(2,128)(2,1)}), bf16[2,128,2,128]{3,2,0,1:T(2,128)(2,1)S(1)}, u32[]{:S(2)}, u32[]{:S(2)}) async-start(bf16[2,128,2,128]{3,2,0,1:T(2,128)(2,1)} %copy.228), calls=%async_computation.5 | async-start | bytes 262144 | tf_op jit(solution)/shard_map/all_to_all | solution.py:125
  266.7 17.2 %all-to-all-start.7 = ((bf16[256,1,2,128]{3,2,1,0:T(2,128)(2,1)}), bf16[256,1,2,128]{3,2,1,0:T(2,128)(2,1)S(1)}, u32[]{:S(2)}, u32[]{:S(2)}) async-start(bf16[256,1,2,128]{3,2,1,0:T(2,128)(2,1)} %copy.243), calls=%async_computation.8 | async-start | bytes 262144 | tf_op jit(solution)/shard_map/all_to_all | solution.py:160
  272.9 51.8 %copy-start.12 = (f32[2,2,128,128]{2,3,1,0:T(8,128)S(1)}, f32[2,2,128,128]{2,3,1,0:T(8,128)}, u32[]{:S(2)}) copy-start(f32[2,2,128,128]{2,3,1,0:T(8,128)} %get-tuple-element.43) | copy-start | bytes 786436
  272.9 51.8 %copy-start.14 = (bf16[2,128,1,2,128]{1,4,3,0,2:T(8,128)(2,1)S(1)}, bf16[2,128,1,2,128]{1,4,3,0,2:T(8,128)(2,1)}, u32[]{:S(2)}) copy-start(bf16[2,128,1,2,128]{1,4,3,0,2:T(8,128)(2,1)} %copy.289) | copy-start | bytes 393220
  283.9 17.2 %all-to-all-start.6 = ((bf16[256,1,2,128]{3,2,1,0:T(2,128)(2,1)}), bf16[256,1,2,128]{3,2,1,0:T(2,128)(2,1)S(1)}, u32[]{:S(2)}, u32[]{:S(2)}) async-start(bf16[256,1,2,128]{3,2,1,0:T(2,128)(2,1)} %copy.235), calls=%async_computation.6 | async-start | bytes 262144 | tf_op jit(solution)/shard_map/all_to_all | solution.py:159
  290.3 45.4 %copy-start.5 = (bf16[2,128,1,2,128]{1,4,3,0,2:T(8,128)(2,1)S(1)}, bf16[2,128,1,2,128]{1,4,3,0,2:T(8,128)(2,1)}, u32[]{:S(2)}) copy-start(bf16[2,128,1,2,128]{1,4,3,0,2:T(8,128)(2,1)} %copy-done.3) | copy-start | bytes 393220
  290.3 45.4 %copy-start.17 = (f32[2,128,2]{1,2,0:T(2,128)S(1)}, f32[2,128,2]{1,2,0:T(2,128)}, u32[]{:S(2)}) copy-start(f32[2,128,2]{1,2,0:T(2,128)} %copy-done.16) | copy-start | bytes 6148
  301.1 17.4 %all-to-all-start.8 = ((bf16[256,1,2,128]{3,2,1,0:T(2,128)(2,1)}), bf16[256,1,2,128]{3,2,1,0:T(2,128)(2,1)S(1)}, u32[]{:S(2)}, u32[]{:S(2)}) async-start(bf16[256,1,2,128]{3,2,1,0:T(2,128)(2,1)} %copy.249), calls=%async_computation.9 | async-start | bytes 262144 | tf_op jit(solution)/shard_map/all_to_all | solution.py:161
  308.3 28.7 %copy-start.2 = (bf16[256,4,2,128]{3,1,0,2:T(4,128)(2,1)S(1)}, bf16[256,4,2,128]{3,1,0,2:T(4,128)(2,1)}, u32[]{:S(2)}) copy-start(bf16[256,4,2,128]{3,1,0,2:T(4,128)(2,1)} %copy-done.1) | copy-start | bytes 1572868
  318.5 17.1 %all-to-all-start.4 = ((bf16[256,1,2,128]{3,2,1,0:T(2,128)(2,1)}), bf16[256,1,2,128]{3,2,1,0:T(2,128)(2,1)S(1)}, u32[]{:S(2)}, u32[]{:S(2)}) async-start(bf16[256,1,2,128]{3,2,1,0:T(2,128)(2,1)} %copy.216), calls=%async_computation.4 | async-start | bytes 262144 | tf_op jit(solution)/shard_map/all_to_all | solution.py:158
  (4 other events, 4.2 us)
Sparse Core Ops, SparseCore 0:
  222.5 569.8 reduce-scatter.1
